TPU v7x, 32 devices: a whole 2x2x4 slice. The times are simulated.
32 devices in a mesh: grid: 8 (over y, x, core), band: 4 (over z).
Axes of the slice: x: 2, y: 2, z: 4, core: 2. Of those that a mesh axis runs over, the one named last changes fastest.
Arguments:
- occupied: bfloat16 [1024, 32, 24, 128], P('band', 'grid'), may hold values from -6 to 6
- potential: float32 [32, 24, 128], P('grid'), may hold values from 0.2 to 4
- shifts: float32 [64], P('band'), may hold values from 0.5 to 4
- source_term: float32 [64, 32, 24, 128], P('band', 'grid'), may hold values from -125 to 125
Outputs:
- solution: float32 [64, 32, 24, 128], P('band', 'grid')
- residual: float32 [64, 32, 24, 128], P('band', 'grid')
All inputs are finite; a program needn't handle non-finite values.
Results may differ from a plain program's by a relative error of at most 0.022.
Values may be sent and summed in bfloat16 or wider, within the bound.
No kernel may reach another device: no remote copies, remote signals or barrier semaphores. Data moves between devices by JAX's collectives and lax.ppermute only.
A program may use at most 128 MiB of HBM per device.

v0:
```python
import math
import jax
import jax.numpy as jnp
from jax import lax
from jax.sharding import PartitionSpec as P

ITERS = 2
COEFFICIENTS = (-205.0 / 72.0, 8.0 / 5.0, -1.0 / 5.0, 8.0 / 315.0, -1.0 / 560.0)


def with_halo(shard, sides, width):
    for axis, dim in sides:
        peers, length = (lax.axis_size(axis), shard.shape[dim])
        up = [(i, (i + 1) % peers) for i in range(peers - 1)]
        down = [(j, i) for i, j in up]
        last = lax.slice_in_dim(shard, length - width, length, axis=dim)
        leading = lax.slice_in_dim(shard, 0, width, axis=dim)
        before = lax.ppermute(last, axis, up)
        after = lax.ppermute(leading, axis, down)
        shard = jnp.concatenate([before, shard, after], axis=dim)
    return shard


def second_sum(padded, extent_x, extent_y, extent_z):
    middle = padded[:, 4 : 4 + extent_x, 4 : 4 + extent_y, 4 : 4 + extent_z]
    summed = 3.0 * COEFFICIENTS[0] * middle
    for offset in range(1, 5):
        along_x = (
            padded[:, 4 + offset : 4 + offset + extent_x, 4 : 4 + extent_y, 4 : 4 + extent_z]
            + padded[:, 4 - offset : 4 - offset + extent_x, 4 : 4 + extent_y, 4 : 4 + extent_z]
        )
        along_y = (
            padded[:, 4 : 4 + extent_x, 4 + offset : 4 + offset + extent_y, 4 : 4 + extent_z]
            + padded[:, 4 : 4 + extent_x, 4 - offset : 4 - offset + extent_y, 4 : 4 + extent_z]
        )
        along_z = (
            padded[:, 4 : 4 + extent_x, 4 : 4 + extent_y, 4 + offset : 4 + offset + extent_z]
            + padded[:, 4 : 4 + extent_x, 4 : 4 + extent_y, 4 - offset : 4 - offset + extent_z]
        )
        summed = (
            summed
            + COEFFICIENTS[offset] * along_x
            + COEFFICIENTS[offset] * along_y
            + COEFFICIENTS[offset] * along_z
        )
    return summed


def inner_product(first_field, second_field):
    return jnp.sum(first_field * second_field, axis=(1, 2, 3))


def expand(vector):
    return vector[:, None, None, None]


def body(occupied, potential, shifts, source_term):
    local_bands, width_x, width_y, width_z = source_term.shape
    local_occupied = occupied.shape[0]
    band_count = lax.axis_size("band")
    local_cells = width_x * width_y * width_z
    weight_scale = 2.0 / math.sqrt(
        local_occupied * band_count * local_cells * lax.axis_size("grid")
    )
    occupied_rows = occupied.reshape(local_occupied, local_cells)
    potential_shift = potential[None] + shifts[:, None, None, None]
    solution = jnp.zeros_like(source_term)
    residual = source_term
    direction = source_term
    norm_now = lax.psum(inner_product(source_term, source_term), "grid")
    for iteration in range(ITERS):
        padded = with_halo(direction.astype(jnp.bfloat16), (("grid", 1),), 4).astype(
            direction.dtype
        )
        padded = jnp.pad(padded, ((0, 0), (0, 0), (4, 4), (4, 4)))
        kinetic = -0.5 * second_sum(padded, width_x, width_y, width_z)
        rounded = direction.astype(jnp.bfloat16).reshape(local_bands, local_cells)
        partial_margin = lax.dot_general(
            occupied_rows,
            lax.all_gather(rounded, "band", axis=0, tiled=True),
            (((1,), (1,)), ((), ())),
            preferred_element_type=jnp.float32,
        )
        margins = lax.psum(partial_margin, "grid")
        scaled = (margins * weight_scale).astype(jnp.bfloat16)
        projected = lax.psum_scatter(
            lax.dot_general(
                scaled, occupied_rows, (((0,), (0,)), ((), ())), preferred_element_type=jnp.float32
            ).astype(jnp.bfloat16),
            "band",
            scatter_dimension=0,
            tiled=True,
        ).astype(jnp.float32)
        applied = kinetic + potential_shift * direction + projected.reshape(direction.shape)
        curvature = lax.psum(inner_product(direction, applied), "grid")
        step_size = norm_now / curvature
        solution = solution + expand(step_size) * direction
        residual = residual - expand(step_size) * applied
        if iteration + 1 < ITERS:
            norm_next = lax.psum(inner_product(residual, residual), "grid")
            direction = residual + expand(norm_next / norm_now) * direction
            norm_now = norm_next
    return (solution, residual)


def solution(mesh):
    in_specs = (
        P("band", "grid", None, None),
        P("grid", None, None),
        P("band"),
        P("band", "grid", None, None),
    )
    out_specs = (P("band", "grid", None, None), P("band", "grid", None, None))
    return jax.shard_map(body, mesh=mesh, in_specs=in_specs, out_specs=out_specs, check_vma=False)
```

profile of v0, /device:TPU:0, one launch (start us, length us, event | category | flops | bytes accessed | tf_op | source)
XLA Modules:
  0.0 345.8 jit_solution(5779249794180429042)
XLA Ops:
  7.2 0.0 all-gather.3.cloned.1.call-start
  7.2 1.2 convert_element_type.31
  8.4 0.9 copy.32
  9.3 0.0 all-gather.3.cloned.1.call-update
  9.3 0.0 all-reduce.6.cloned.1.call-start
  9.4 40.6 %all-gather.3.cloned.1.call-done = bf16[64,12288]{1,0:T(8,128)(2,1)} async-done(((bf16[16,12288]{1,0:T(8,128)(2,1)}), bf16[64,12288]{1,0:T(8,128)(2,1)}) %all-gather.3.cloned.1.call-update) | async-done | bytes 1572880 | tf_op jit(solution)/shard_map/all_gather | solution.py:80
  50.0 5.8 %fusion.4 = f32[256,64]{1,0:T(8,128)} fusion(bf16[64,12288]{1,0:T(8,128)(2,1)} %all-gather.3.cloned.1.call-done, bf16[32,8,96,128]{3,2,1,0:T(8,128)(2,1)} %bitcast.35), kind=kOutput, calls=%fused_computation.38 | convolution fusion | flops 402653184 | bytes 7929856 | tf_op jit(solution)/shard_map/dot_general | solution.py:78
  55.8 0.0 all-reduce.6.cloned.1.call-update
  55.8 0.0 reduce-scatter.3.cloned.1.call-start
  55.9 51.9 %all-reduce.6.cloned.1.call-done = f32[256,64]{1,0:T(8,128)} async-done(((f32[256,64]{1,0:T(8,128)}), f32[256,64]{1,0:T(8,128)}) %all-reduce.6.cloned.1.call-update) | async-done | bytes 65552 | tf_op jit(solution)/shard_map/psum | solution.py:84
  107.8 6.2 %convolution_convert_fusion.1 = bf16[64,12288]{1,0:T(8,128)(2,1)} fusion(bf16[32,8,96,128]{3,2,1,0:T(8,128)(2,1)} %bitcast.36, f32[256,64]{1,0:T(8,128)} %all-reduce.6.cloned.1.call-done), kind=kOutput, calls=%fused_computation.33 | convolution fusion | flops 403472384 | bytes 7929856 | tf_op jit(solution)/shard_map/dot_general | solution.py:87
  113.9 0.0 reduce-scatter.3.cloned.1.call-update
  113.9 0.0 copy-start
  114.0 0.0 copy-start.2
  114.0 0.0 all-gather.5.cloned.1.call-start
  114.0 1.4 collective-permute-start.1
  115.5 3.1 collective-permute-start
  118.5 1.3 collective-permute-done
  119.8 0.2 maximum_convert_fusion
  120.0 28.8 %reduce-scatter.3.cloned.1.call-done = bf16[16,12288]{1,0:T(8,128)(2,1)} async-done(((bf16[64,12288]{1,0:T(8,128)(2,1)}), bf16[16,12288]{1,0:T(8,128)(2,1)}) %reduce-scatter.3.cloned.1.call-update) | async-done | bytes 393232 | tf_op jit(solution)/shard_map/reduce_scatter | solution.py:86
  148.8 1.0 convert_bitcast_fusion.1
  149.8 0.2 copy.8
  150.0 3.8 %multiply_reduce_fusion.2 = (f32[16]{0:T(128)S(1)}, f32[16]{0:T(128)S(1)}, f32[16,4,24,128]{3,2,1,0:T(8,128)}) fusion(f32[16,4,24,128]{3,2,1,0:T(8,128)S(1)} %copy-done, f32[16,4,24,128]{3,2,1,0:T(8,128)S(1)} %bitcast.41, f32[16]{0:T(128)S(1)} %copy-done.2, f32[4,24,128]{2,1,0:T(8,128)} %param.5, f32[16,12,24,128]{3,2,1,0:T(8,128)S(1)} %maximum_convert_fusion), kind=kLoop, calls=%fused_computation.135 | loop fusion | flops 9043936 | bytes 11846272 | tf_op jit(solution)/shard_map/reduce_sum | solution.py:50
  153.8 13.4 %all-reduce.2 = (f32[16]{0:T(128)S(1)}, f32[16]{0:T(128)S(1)}) all-reduce(f32[16]{0:T(128)S(1)} %get-tuple-element.3, f32[16]{0:T(128)S(1)} %get-tuple-element.2), channel_id=1, replica_groups=mesh['grid'=8,'band'=4] {'grid'}, use_global_device_ids=true, to_apply=%region_1.0 | all-reduce | flops 32 | bytes 256 | tf_op jit(solution)/shard_map/psum | solution.py:70
  167.3 1.4 multiply_reduce_fusion.1
  168.7 11.8 %psum.45 = f32[16]{0:T(128)S(1)} all-reduce(f32[16]{0:T(128)S(1)} %multiply_reduce_fusion.1), channel_id=1, replica_groups=mesh['grid'=8,'band'=4] {'grid'}, use_global_device_ids=true, to_apply=%region_7.8 | all-reduce | flops 16 | bytes 128 | tf_op jit(solution)/shard_map/psum | solution.py:100
  180.5 2.3 fusion.86
  182.8 0.9 copy.31
  183.7 0.0 all-gather.5.cloned.1.call-update
  183.7 0.0 all-reduce.8.cloned.1.call-start
  183.7 34.6 %all-gather.5.cloned.1.call-done = bf16[64,12288]{1,0:T(8,128)(2,1)} async-done(((bf16[16,12288]{1,0:T(8,128)(2,1)}), bf16[64,12288]{1,0:T(8,128)(2,1)}) %all-gather.5.cloned.1.call-update) | async-done | bytes 1572880 | tf_op jit(solution)/shard_map/all_gather | solution.py:80
  218.3 5.9 %fusion.10 = f32[256,64]{1,0:T(8,128)} fusion(bf16[64,12288]{1,0:T(8,128)(2,1)} %all-gather.5.cloned.1.call-done, bf16[32,8,96,128]{3,2,1,0:T(8,128)(2,1)} %bitcast.37), kind=kOutput, calls=%fused_computation.46 | convolution fusion | flops 402653184 | bytes 7929856 | tf_op jit(solution)/shard_map/dot_general | solution.py:78
  224.2 0.0 all-reduce.8.cloned.1.call-update
  224.2 0.0 reduce-scatter.5.cloned.1.call-start
  224.3 51.9 %all-reduce.8.cloned.1.call-done = f32[256,64]{1,0:T(8,128)} async-done(((f32[256,64]{1,0:T(8,128)}), f32[256,64]{1,0:T(8,128)}) %all-reduce.8.cloned.1.call-update) | async-done | bytes 65552 | tf_op jit(solution)/shard_map/psum | solution.py:84
  276.2 6.2 %convolution_convert_fusion = bf16[64,12288]{1,0:T(8,128)(2,1)} fusion(bf16[32,8,96,128]{3,2,1,0:T(8,128)(2,1)} %bitcast.38, f32[256,64]{1,0:T(8,128)} %all-reduce.8.cloned.1.call-done), kind=kOutput, calls=%fused_computation.32 | convolution fusion | flops 403472384 | bytes 7929856 | tf_op jit(solution)/shard_map/dot_general | solution.py:87
  282.3 0.0 reduce-scatter.5.cloned.1.call-update
  282.4 1.3 collective-permute-start.3
  283.7 3.1 collective-permute-start.2
  286.7 0.0 collective-permute-done.3
  286.7 1.3 collective-permute-done.2
  288.0 0.2 maximum_convert_fusion.1
  288.2 29.0 %reduce-scatter.5.cloned.1.call-done = bf16[16,12288]{1,0:T(8,128)(2,1)} async-done(((bf16[64,12288]{1,0:T(8,128)(2,1)}), bf16[16,12288]{1,0:T(8,128)(2,1)}) %reduce-scatter.5.cloned.1.call-update) | async-done | bytes 393232 | tf_op jit(solution)/shard_map/reduce_scatter | solution.py:86
  317.2 1.1 convert_bitcast_fusion
  318.3 0.2 copy.10
  318.5 3.9 %multiply_reduce_fusion = (f32[16]{0:T(128)S(1)}, f32[16,4,24,128]{3,2,1,0:T(8,128)}) fusion(f32[16,4,24,128]{3,2,1,0:T(8,128)S(1)} %copy-done.1, f32[16,4,24,128]{3,2,1,0:T(8,128)S(1)} %bitcast.42, f32[16]{0:T(128)S(1)} %copy-done.2, f32[4,24,128]{2,1,0:T(8,128)} %param.5, f32[16,12,24,128]{3,2,1,0:T(8,128)S(1)} %maximum_convert_fusion.1), kind=kLoop, calls=%fused_computation.131 | loop fusion | flops 8650736 | bytes 11846208 | tf_op jit(solution)/shard_map/reduce_sum | solution.py:50
  322.3 13.4 %psum.47 = f32[16]{0:T(128)S(1)} all-reduce(f32[16]{0:T(128)S(1)} %get-tuple-element.6), channel_id=1, replica_groups=mesh['grid'=8,'band'=4] {'grid'}, use_global_device_ids=true, to_apply=%region_11.12 | all-reduce | flops 16 | bytes 128 | tf_op jit(solution)/shard_map/psum | solution.py:95
  335.8 3.2 multiply_subtract_fusion
  (8 shorter events, 0.0 us)
Async XLA Ops:
  7.2 42.8 %all-gather.3.cloned.1.call-start = ((), (), s32[]{:S(2)}) async-start(), calls=%async_computation.2 | async-start | bytes 1966080 | tf_op jit(solution)/shard_map/all_gather | solution.py:80
  9.3 98.4 %all-reduce.6.cloned.1.call-start = ((), (), s32[]{:S(2)}) async-start(), calls=%async_computation.3 | async-start | bytes 262144 | tf_op jit(solution)/shard_map/psum | solution.py:84
  55.8 92.9 %reduce-scatter.3.cloned.1.call-start = ((), (), s32[]{:S(2)}) async-start(), calls=%async_computation.4 | async-start | bytes 1966080 | tf_op jit(solution)/shard_map/reduce_scatter | solution.py:86
  113.9 36.0 %copy-start = (f32[16,4,24,128]{3,2,1,0:T(8,128)S(1)}, f32[16,4,24,128]{3,2,1,0:T(8,128)}, u32[]{:S(2)}) copy-start(f32[16,4,24,128]{3,2,1,0:T(8,128)} %param.7) | copy-start | bytes 2359300
  114.0 36.0 %copy-start.2 = (f32[16]{0:T(128)S(1)}, f32[16]{0:T(128)}, u32[]{:S(2)}) copy-start(f32[16]{0:T(128)} %param.6) | copy-start | bytes 196
  114.0 104.4 %all-gather.5.cloned.1.call-start = ((), (), s32[]{:S(2)}) async-start(), calls=%async_computation.5 | async-start | bytes 1966080 | tf_op jit(solution)/shard_map/all_gather | solution.py:80
  114.0 4.5 %collective-permute-start.1 = (bf16[16,4,24,128]{3,2,1,0:T(8,128)(2,1)S(1)}, bf16[16,4,24,128]{3,2,1,0:T(8,128)(2,1)S(1)}, u32[]{:S(2)}, u32[]{:S(2)}) collective-permute-start(bf16[16,4,24,128]{3,2,1,0:T(8,128)(2,1)S(1)} %convert_element_type.31), channel_id=1, source_target_pairs={{4,0},{8,4},{12,8},{16,12},{20,16},{24,20},{28,24},{5,1},{9,5},{13... | collective-permute-start | bytes 1179656 | tf_op jit(solution)/shard_map/ppermute | solution.py:19
  115.5 4.4 %collective-permute-start = (bf16[16,4,24,128]{3,2,1,0:T(8,128)(2,1)S(1)}, bf16[16,4,24,128]{3,2,1,0:T(8,128)(2,1)S(1)}, u32[]{:S(2)}, u32[]{:S(2)}) collective-permute-start(bf16[16,4,24,128]{3,2,1,0:T(8,128)(2,1)S(1)} %convert_element_type.31), channel_id=1, source_target_pairs={{0,4},{4,8},{8,12},{12,16},{16,20},{20,24},{24,28},{1,5},{5,9},{9,... | collective-permute-start | bytes 1179656 | tf_op jit(solution)/shard_map/ppermute | solution.py:18
  183.7 92.5 %all-reduce.8.cloned.1.call-start = ((), (), s32[]{:S(2)}) async-start(), calls=%async_computation.6 | async-start | bytes 262144 | tf_op jit(solution)/shard_map/psum | solution.py:84
  224.2 93.0 %reduce-scatter.5.cloned.1.call-start = ((), (), s32[]{:S(2)}) async-start(), calls=%async_computation.7 | async-start | bytes 1966080 | tf_op jit(solution)/shard_map/reduce_scatter | solution.py:86
  282.4 4.4 %collective-permute-start.3 = (bf16[16,4,24,128]{3,2,1,0:T(8,128)(2,1)S(1)}, bf16[16,4,24,128]{3,2,1,0:T(8,128)(2,1)S(1)}, u32[]{:S(2)}, u32[]{:S(2)}) collective-permute-start(bf16[16,4,24,128]{3,2,1,0:T(8,128)(2,1)S(1)} %get-tuple-element.8), channel_id=1, source_target_pairs={{4,0},{8,4},{12,8},{16,12},{20,16},{24,20},{28,24},{5,1},{9,5},{13... | collective-permute-start | bytes 1179656 | tf_op jit(solution)/shard_map/ppermute | solution.py:19
  283.7 4.4 %collective-permute-start.2 = (bf16[16,4,24,128]{3,2,1,0:T(8,128)(2,1)S(1)}, bf16[16,4,24,128]{3,2,1,0:T(8,128)(2,1)S(1)}, u32[]{:S(2)}, u32[]{:S(2)}) collective-permute-start(bf16[16,4,24,128]{3,2,1,0:T(8,128)(2,1)S(1)} %get-tuple-element.8), channel_id=1, source_target_pairs={{0,4},{4,8},{8,12},{12,16},{16,20},{20,24},{24,28},{1,5},{5,9},{9,... | collective-permute-start | bytes 1179656 | tf_op jit(solution)/shard_map/ppermute | solution.py:18
  317.2 1.3 copy-start.1
Sparse Core Ops, SparseCore 0:
  10.1 39.7 all-gather.2
  56.0 51.7 all-reduce.5
  114.1 34.6 reduce-scatter.2
  183.8 34.4 all-gather.4
  224.4 51.7 all-reduce.7
  282.5 34.6 reduce-scatter.4
where the time goes:
time: 346 us
  waiting for transfers between devices  239 us (69%)
  blocking collectives  38.6 us (11%)
  matrix products  24 us (7%)
  other arithmetic  18.3 us (5%)
  between operations  14.2 us (4%)
  starting transfers between devices  9.07 us (3%)
    psum x2, waiting for transfers between devices, body(): margins = lax.psum(partial_margin, 'grid')  104 us
    all_gather x2, waiting for transfers between devices, body(): lax.all_gather(rounded, 'band', axis=0, tiled=True)  75.2 us
    reduce_scatter x2, waiting for transfers between devices, body(): lax.psum_scatter(lax.dot_general(scaled, occupied_rows, (((0,), (0,)), ((...  57.8 us
    psum x1, blocking collectives, body(): curvature = lax.psum(inner_product(direction, applied), 'grid')  13.4 us
    psum x1, blocking collectives, body(): norm_now = lax.psum(inner_product(source_term, source_term), 'grid')  13.4 us
    dot_general x2, matrix products, body(): lax.dot_general(scaled, occupied_rows, (((0,), (0,)), ((), ())), preferre...  12.3 us
    psum x1, blocking collectives, body(): norm_next = lax.psum(inner_product(residual, residual), 'grid')  11.8 us
    dot_general x2, matrix products, body(): lax.dot_general(occupied_rows, lax.all_gather(rounded, 'band', axis=0, ti...  11.7 us
  transfers between devices with their start and end apart: 10, of which 8 were waited for; matrix products, arithmetic and copies ran while one was open for 0% of the time, Pallas kernels for 0%

commit v1 on v0

--- a/solution.py
+++ b/solution.py
@@ -6,6 +6,27 @@
 
 ITERS = 2
 COEFFICIENTS = (-205.0 / 72.0, 8.0 / 5.0, -1.0 / 5.0, 8.0 / 315.0, -1.0 / 560.0)
+
+
+def joined_along(blocks, dim):
+    blocks = jnp.moveaxis(blocks, 0, dim)
+    shape = blocks.shape
+    return blocks.reshape(*shape[:dim], shape[dim] * shape[dim + 1], *shape[dim + 2 :])
+
+
+def grow_blocks(x, axis):
+    size, here = (lax.axis_size(axis), lax.axis_index(axis))
+    blocks, stride = (x[None], 1)
+    while stride < size:
+        theirs = lax.ppermute(blocks, axis, [(i, i ^ stride) for i in range(size)])
+        low = here & stride == 0
+        blocks = jnp.concatenate([jnp.where(low, blocks, theirs), jnp.where(low, theirs, blocks)])
+        stride *= 2
+    return blocks
+
+
+def collect(shard, axis, dim):
+    return joined_along(grow_blocks(shard, axis), dim)
 
 
 def with_halo(shard, sides, width):
@@ -77,7 +98,7 @@
         rounded = direction.astype(jnp.bfloat16).reshape(local_bands, local_cells)
         partial_margin = lax.dot_general(
             occupied_rows,
-            lax.all_gather(rounded, "band", axis=0, tiled=True),
+            collect(rounded, "band", 0),
             (((1,), (1,)), ((), ())),
             preferred_element_type=jnp.float32,
         )

time: 346 us -> 363 us (1.049)
  waiting for transfers between devices: 239 us -> 253 us
  starting transfers between devices: 9.07 us -> 16.6 us
  matrix products: 24 us -> 17.9 us
    ppermute x0 -> x4, waiting for transfers between devices: none -> 88.5 us  [grow_blocks(): theirs = lax.ppermute(blocks, axis, [(i, i ^ stride) for i in range(size)])]
    all_gather x2 -> x0, waiting for transfers between devices: 75.2 us -> none  [body(): lax.all_gather(rounded, 'band', axis=0, tiled=True)]
    ppermute x0 -> x4, starting transfers between devices: none -> 7.6 us  [grow_blocks(): theirs = lax.ppermute(blocks, axis, [(i, i ^ stride) for i in range(size)])]
    dot_general x2, matrix products: 11.7 us -> 5.66 us  [body(): lax.dot_general(occupied_rows, collect(rounded, 'band', 0), (((1,), (1,))...]
  transfers between devices with their start and end apart: 10 -> 12, of which waited for: 8 -> 10; matrix products, arithmetic and copies ran while one was open for 0% -> 0% of each run, Pallas kernels for 0% -> 0%
where the time goes in v1:
time: 363 us; the launch traced here: 362 us
  waiting for transfers between devices  253 us (70%)
  blocking collectives  38.6 us (11%)
  other arithmetic  18.6 us (5%)
  matrix products  17.9 us (5%)
  starting transfers between devices  16.6 us (5%)
  between operations  14 us (4%)
  local copies, waits for them, and re-layouts  3.97 us (1%)
    psum x2, waiting for transfers between devices, body(): margins = lax.psum(partial_margin, 'grid')  104 us
    ppermute x4, waiting for transfers between devices, grow_blocks(): theirs = lax.ppermute(blocks, axis, [(i, i ^ stride) for i in range(size)])  88.5 us
    reduce_scatter x2, waiting for transfers between devices, body(): lax.psum_scatter(lax.dot_general(scaled, occupied_rows, (((0,), (0,)), ((...  57.9 us
    psum x1, blocking collectives, body(): curvature = lax.psum(inner_product(direction, applied), 'grid')  13.4 us
    psum x1, blocking collectives, body(): norm_now = lax.psum(inner_product(source_term, source_term), 'grid')  13.4 us
    dot_general x2, matrix products, body(): lax.dot_general(scaled, occupied_rows, (((0,), (0,)), ((), ())), preferre...  12.3 us
    psum x1, blocking collectives, body(): norm_next = lax.psum(inner_product(residual, residual), 'grid')  11.8 us
    ppermute x4, starting transfers between devices, grow_blocks(): theirs = lax.ppermute(blocks, axis, [(i, i ^ stride) for i in range(size)])  7.6 us
  transfers between devices with their start and end apart: 12, of which 10 were waited for; matrix products, arithmetic and copies ran while one was open for 0% of the time, Pallas kernels for 0%

profile of v1, /device:TPU:0, one launch (start us, length us, event | category | flops | bytes accessed | tf_op | source)
XLA Modules:
  0.0 362.4 jit_solution(9853384434465774333)
XLA Ops:
  7.2 1.2 convert_element_type.31
  8.4 0.2 broadcast_in_dim_reshape.6
  8.6 3.1 collective-permute-start.2
  11.7 9.1 %collective-permute-done.2 = bf16[1,16,12288]{2,1,0:T(8,128)(2,1)S(1)} collective-permute-done((bf16[1,16,12288]{2,1,0:T(8,128)(2,1)S(1)}, bf16[1,16,12288]{2,1,0:T(8,128)(2,1)S(1)}, u32[]{:S(2)}, u32[]{:S(2)}) %collective-permute-start.2) | collective-permute-done | bytes 393248 | tf_op jit(solution)/shard_map/ppermute | solution.py:21
  20.8 0.1 broadcast_select_fusion.7
  20.8 0.1 pad_maximum_fusion.2
  20.9 2.8 collective-permute-start.3
  23.7 33.7 %collective-permute-done.3 = bf16[2,16,12288]{2,1,0:T(8,128)(2,1)S(1)} collective-permute-done((bf16[2,16,12288]{2,1,0:T(8,128)(2,1)S(1)}, bf16[2,16,12288]{2,1,0:T(8,128)(2,1)S(1)}, u32[]{:S(2)}, u32[]{:S(2)}) %collective-permute-start.3) | collective-permute-done | bytes 786464 | tf_op jit(solution)/shard_map/ppermute | solution.py:21
  57.5 0.1 broadcast_select_fusion.3
  57.6 0.1 pad_maximum_fusion
  57.7 2.5 copy-done
  60.3 2.8 fusion.10
  63.1 53.6 %all-reduce.6.cloned.1.call-done = f32[256,64]{0,1:T(8,128)} async-done(((f32[256,64]{0,1:T(8,128)}), f32[256,64]{0,1:T(8,128)}) %all-reduce.6.cloned.1.call-update) | async-done | bytes 65552 | tf_op jit(solution)/shard_map/psum | solution.py:105
  116.7 6.1 %convolution_convert_fusion.1 = bf16[64,12288]{1,0:T(8,128)(2,1)} fusion(bf16[32,8,96,128]{3,2,1,0:T(8,128)(2,1)} %bitcast.35, f32[256,64]{0,1:T(8,128)} %all-reduce.6.cloned.1.call-done), kind=kOutput, calls=%fused_computation.33 | convolution fusion | flops 403472384 | bytes 7929856 | tf_op jit(solution)/shard_map/dot_general | solution.py:108
  122.9 1.3 collective-permute-start.1
  124.2 3.1 collective-permute-start
  127.3 1.3 collective-permute-done
  128.6 0.2 maximum_convert_fusion
  128.8 28.9 %reduce-scatter.3.cloned.1.call-done = bf16[16,12288]{1,0:T(8,128)(2,1)} async-done(((bf16[64,12288]{1,0:T(8,128)(2,1)}), bf16[16,12288]{1,0:T(8,128)(2,1)}) %reduce-scatter.3.cloned.1.call-update) | async-done | bytes 393232 | tf_op jit(solution)/shard_map/reduce_scatter | solution.py:107
  157.7 1.0 convert_bitcast_fusion.1
  158.7 0.2 copy.7
  158.9 3.0 multiply_reduce_fusion.2
  162.0 13.4 %all-reduce.2 = (f32[16]{0:T(128)S(1)}, f32[16]{0:T(128)S(1)}) all-reduce(f32[16]{0:T(128)S(1)} %get-tuple-element.3, f32[16]{0:T(128)S(1)} %get-tuple-element.2), channel_id=1, replica_groups=mesh['grid'=8,'band'=4] {'grid'}, use_global_device_ids=true, to_apply=%region_1.0 | all-reduce | flops 32 | bytes 256 | tf_op jit(solution)/shard_map/psum | solution.py:91
  175.4 1.4 multiply_reduce_fusion.1
  176.8 11.8 %psum.45 = f32[16]{0:T(128)S(1)} all-reduce(f32[16]{0:T(128)S(1)} %multiply_reduce_fusion.1), channel_id=1, replica_groups=mesh['grid'=8,'band'=4] {'grid'}, use_global_device_ids=true, to_apply=%region_7.8 | all-reduce | flops 16 | bytes 128 | tf_op jit(solution)/shard_map/psum | solution.py:121
  188.6 2.4 fusion.89
  191.1 0.9 broadcast_in_dim_reshape.7
  192.0 11.1 %collective-permute-done.6 = bf16[1,16,12288]{2,1,0:T(8,128)(2,1)S(1)} collective-permute-done((bf16[1,16,12288]{2,1,0:T(8,128)(2,1)}, bf16[1,16,12288]{2,1,0:T(8,128)(2,1)S(1)}, u32[]{:S(2)}, u32[]{:S(2)}) %collective-permute-start.6) | collective-permute-done | bytes 393248 | tf_op jit(solution)/shard_map/ppermute | solution.py:21
  203.1 1.1 broadcast_select_fusion.5
  204.1 0.1 pad_maximum_fusion.3
  204.2 1.7 collective-permute-start.7
  205.9 34.6 %collective-permute-done.7 = bf16[2,16,12288]{2,1,0:T(8,128)(2,1)S(1)} collective-permute-done((bf16[2,16,12288]{2,1,0:T(8,128)(2,1)S(1)}, bf16[2,16,12288]{2,1,0:T(8,128)(2,1)S(1)}, u32[]{:S(2)}, u32[]{:S(2)}) %collective-permute-start.7) | collective-permute-done | bytes 786464 | tf_op jit(solution)/shard_map/ppermute | solution.py:21
  240.5 0.1 broadcast_select_fusion.1
  240.6 0.1 pad_maximum_fusion.1
  240.8 2.9 fusion.13
  243.7 0.2 reduce-scatter.5.cloned.1.call-start
  243.9 50.0 %all-reduce.8.cloned.1.call-done = f32[256,64]{0,1:T(8,128)} async-done(((f32[256,64]{0,1:T(8,128)}), f32[256,64]{0,1:T(8,128)}) %all-reduce.8.cloned.1.call-update) | async-done | bytes 65552 | tf_op jit(solution)/shard_map/psum | solution.py:105
  293.9 6.1 %convolution_convert_fusion = bf16[64,12288]{1,0:T(8,128)(2,1)} fusion(bf16[32,8,96,128]{3,2,1,0:T(8,128)(2,1)} %bitcast.36, f32[256,64]{0,1:T(8,128)} %all-reduce.8.cloned.1.call-done), kind=kOutput, calls=%fused_computation.32 | convolution fusion | flops 403472384 | bytes 7929856 | tf_op jit(solution)/shard_map/dot_general | solution.py:108
  300.0 1.3 collective-permute-start.5
  301.3 3.1 collective-permute-start.4
  304.4 1.3 collective-permute-done.4
  305.7 0.2 maximum_convert_fusion.1
  305.9 29.0 %reduce-scatter.5.cloned.1.call-done = bf16[16,12288]{1,0:T(8,128)(2,1)} async-done(((bf16[64,12288]{1,0:T(8,128)(2,1)}), bf16[16,12288]{1,0:T(8,128)(2,1)}) %reduce-scatter.5.cloned.1.call-update) | async-done | bytes 393232 | tf_op jit(solution)/shard_map/reduce_scatter | solution.py:107
  334.9 1.1 convert_bitcast_fusion
  336.0 0.2 copy.8
  336.2 3.1 multiply_reduce_fusion
  339.3 13.4 %psum.47 = f32[16]{0:T(128)S(1)} all-reduce(f32[16]{0:T(128)S(1)} %get-tuple-element.6), channel_id=1, replica_groups=mesh['grid'=8,'band'=4] {'grid'}, use_global_device_ids=true, to_apply=%region_11.12 | all-reduce | flops 16 | bytes 128 | tf_op jit(solution)/shard_map/psum | solution.py:116
  352.7 3.2 multiply_subtract_fusion
  (29 shorter events, 0.3 us)
Async XLA Ops:
  7.2 109.5 %all-reduce.6.cloned.1.call-start = ((), (), s32[]{:S(2)}) async-start(), calls=%async_computation.2 | async-start | bytes 131072 | tf_op jit(solution)/shard_map/psum | solution.py:105
  8.6 12.2 %collective-permute-start.2 = (bf16[1,16,12288]{2,1,0:T(8,128)(2,1)S(1)}, bf16[1,16,12288]{2,1,0:T(8,128)(2,1)S(1)}, u32[]{:S(2)}, u32[]{:S(2)}) collective-permute-start(bf16[1,16,12288]{2,1,0:T(8,128)(2,1)S(1)} %broadcast_in_dim_reshape.6), channel_id=1, source_target_pairs={{0,1},{1,0},{2,3},{3,2},{4,5},{5,4},{6,7},{7,6},{8,9},{9,8},{10,11... | collective-permute-start | bytes 1179656 | tf_op jit(solution)/shard_map/ppermute | solution.py:21
  20.9 36.5 %collective-permute-start.3 = (bf16[2,16,12288]{2,1,0:T(8,128)(2,1)S(1)}, bf16[2,16,12288]{2,1,0:T(8,128)(2,1)S(1)}, u32[]{:S(2)}, u32[]{:S(2)}) collective-permute-start(bf16[2,16,12288]{2,1,0:T(8,128)(2,1)S(1)} %pad_maximum_fusion.2), channel_id=1, source_target_pairs={{0,2},{1,3},{2,0},{3,1},{4,6},{5,7},{6,4},{7,5},{8,10},{9,11},{10,... | collective-permute-start | bytes 2359304 | tf_op jit(solution)/shard_map/ppermute | solution.py:21
  57.5 2.8 copy-start
  63.1 94.6 %reduce-scatter.3.cloned.1.call-start = ((), (), s32[]{:S(2)}) async-start(), calls=%async_computation.3 | async-start | bytes 1966080 | tf_op jit(solution)/shard_map/reduce_scatter | solution.py:107
  122.8 171.0 %all-reduce.8.cloned.1.call-start = ((), (), s32[]{:S(2)}) async-start(), calls=%async_computation.4 | async-start | bytes 131072 | tf_op jit(solution)/shard_map/psum | solution.py:105
  122.9 4.4 %collective-permute-start.1 = (bf16[16,4,24,128]{3,2,1,0:T(8,128)(2,1)S(1)}, bf16[16,4,24,128]{3,2,1,0:T(8,128)(2,1)S(1)}, u32[]{:S(2)}, u32[]{:S(2)}) collective-permute-start(bf16[16,4,24,128]{3,2,1,0:T(8,128)(2,1)S(1)} %convert_element_type.31), channel_id=1, source_target_pairs={{4,0},{8,4},{12,8},{16,12},{20,16},{24,20},{28,24},{5,1},{9,5},{13... | collective-permute-start | bytes 1179656 | tf_op jit(solution)/shard_map/ppermute | solution.py:40
  124.2 4.4 %collective-permute-start = (bf16[16,4,24,128]{3,2,1,0:T(8,128)(2,1)S(1)}, bf16[16,4,24,128]{3,2,1,0:T(8,128)(2,1)S(1)}, u32[]{:S(2)}, u32[]{:S(2)}) collective-permute-start(bf16[16,4,24,128]{3,2,1,0:T(8,128)(2,1)S(1)} %convert_element_type.31), channel_id=1, source_target_pairs={{0,4},{4,8},{8,12},{12,16},{16,20},{20,24},{24,28},{1,5},{5,9},{9,... | collective-permute-start | bytes 1179656 | tf_op jit(solution)/shard_map/ppermute | solution.py:39
  128.7 30.2 %copy-start.1 = (f32[16,4,24,128]{3,2,1,0:T(8,128)S(1)}, f32[16,4,24,128]{3,2,1,0:T(8,128)}, u32[]{:S(2)}) copy-start(f32[16,4,24,128]{3,2,1,0:T(8,128)} %param.7) | copy-start | bytes 2359300
  128.7 30.2 %copy-start.3 = (f32[4,24,128]{2,1,0:T(8,128)S(1)}, f32[4,24,128]{2,1,0:T(8,128)}, u32[]{:S(2)}) copy-start(f32[4,24,128]{2,1,0:T(8,128)} %param.5) | copy-start | bytes 147460
  128.8 30.2 %copy-start.5 = (f32[16]{0:T(128)S(1)}, f32[16]{0:T(128)}, u32[]{:S(2)}) copy-start(f32[16]{0:T(128)} %param.6) | copy-start | bytes 196
  188.6 52.1 %slice-start = ((s8[6291456]{0:T(1024)(128)(4,1)}), s8[2097152]{0:T(1024)(128)(4,1)S(1)}, s32[]{:S(2)}) async-start(s8[6291456]{0:T(1024)(128)(4,1)} %bitcast.38), calls=%async_computation.6 | async-start | bytes 4194304
  192.0 11.1 %collective-permute-start.6 = (bf16[1,16,12288]{2,1,0:T(8,128)(2,1)}, bf16[1,16,12288]{2,1,0:T(8,128)(2,1)S(1)}, u32[]{:S(2)}, u32[]{:S(2)}) collective-permute-start(bf16[1,16,12288]{2,1,0:T(8,128)(2,1)} %broadcast_in_dim_reshape.7), channel_id=1, source_target_pairs={{0,1},{1,0},{2,3},{3,2},{4,5},{5,4},{6,7},{7,6},{8,9},{9,8},{10,11... | collective-permute-start | bytes 1179656 | tf_op jit(solution)/shard_map/ppermute | solution.py:21
  204.1 36.6 %slice-start.1 = ((s8[6291456]{0:T(1024)(128)(4,1)}), s8[4194304]{0:T(1024)(128)(4,1)S(1)}, s32[]{:S(2)}) async-start(s8[6291456]{0:T(1024)(128)(4,1)} %bitcast.38), calls=%async_computation.7 | async-start | bytes 8388608
  204.2 36.3 %collective-permute-start.7 = (bf16[2,16,12288]{2,1,0:T(8,128)(2,1)S(1)}, bf16[2,16,12288]{2,1,0:T(8,128)(2,1)S(1)}, u32[]{:S(2)}, u32[]{:S(2)}) collective-permute-start(bf16[2,16,12288]{2,1,0:T(8,128)(2,1)S(1)} %pad_maximum_fusion.3), channel_id=1, source_target_pairs={{0,2},{1,3},{2,0},{3,1},{4,6},{5,7},{6,4},{7,5},{8,10},{9,11},{10,... | collective-permute-start | bytes 2359304 | tf_op jit(solution)/shard_map/ppermute | solution.py:21
  243.7 91.2 %reduce-scatter.5.cloned.1.call-start = ((), (), s32[]{:S(2)}) async-start(), calls=%async_computation.5 | async-start | bytes 1966080 | tf_op jit(solution)/shard_map/reduce_scatter | solution.py:107
  300.0 4.4 %collective-permute-start.5 = (bf16[16,4,24,128]{3,2,1,0:T(8,128)(2,1)S(1)}, bf16[16,4,24,128]{3,2,1,0:T(8,128)(2,1)S(1)}, u32[]{:S(2)}, u32[]{:S(2)}) collective-permute-start(bf16[16,4,24,128]{3,2,1,0:T(8,128)(2,1)S(1)} %get-tuple-element.8), channel_id=1, source_target_pairs={{4,0},{8,4},{12,8},{16,12},{20,16},{24,20},{28,24},{5,1},{9,5},{13... | collective-permute-start | bytes 1179656 | tf_op jit(solution)/shard_map/ppermute | solution.py:40
  301.3 4.4 %collective-permute-start.4 = (bf16[16,4,24,128]{3,2,1,0:T(8,128)(2,1)S(1)}, bf16[16,4,24,128]{3,2,1,0:T(8,128)(2,1)S(1)}, u32[]{:S(2)}, u32[]{:S(2)}) collective-permute-start(bf16[16,4,24,128]{3,2,1,0:T(8,128)(2,1)S(1)} %get-tuple-element.8), channel_id=1, source_target_pairs={{0,4},{4,8},{8,12},{12,16},{16,20},{20,24},{24,28},{1,5},{5,9},{9,... | collective-permute-start | bytes 1179656 | tf_op jit(solution)/shard_map/ppermute | solution.py:39
  305.9 30.3 %copy-start.4 = (f32[4,24,128]{2,1,0:T(8,128)S(1)}, f32[4,24,128]{2,1,0:T(8,128)}, u32[]{:S(2)}) copy-start(f32[4,24,128]{2,1,0:T(8,128)} %param.5) | copy-start | bytes 147460
  334.9 1.3 copy-start.2
Sparse Core Ops, SparseCore 0:
  63.2 53.4 all-reduce.5
  123.0 34.6 reduce-scatter.2
  243.8 50.0 all-reduce.7
  300.1 34.6 reduce-scatter.4
